TPU v7x, 512 devices: a whole 4x4x16 slice. The times are simulated.
512 devices in a mesh: dp: 32 (over y_hi, z), tensor: 16 (over x, y_lo, core).
Axes of the slice: x: 4, y: 4 (y_hi: 2, y_lo: 2; y = y_hi * 2 + y_lo), z: 16, core: 2. Of those that a mesh axis runs over, the one named last changes fastest.
Arguments:
- residual: bfloat16 [65536, 2048], P(('dp', 'tensor')), may hold values from -0.59765625 to 0.59765625
- queries: bfloat16 [65536, 2048], P(('dp', 'tensor')), may hold values from -27 to 27
- new_keys: bfloat16 [65536, 2048], P(('dp', 'tensor')), may hold values from -27 to 27
- new_values: bfloat16 [65536, 2048], P(('dp', 'tensor')), may hold values from -6 to 6
- lengths: int32 [32, 2], P('dp'), may hold values from 1 to 1536, 2048 in all within a row
- page_order: int32 [32, 17], P('dp'), may hold values from 0 to 16, each once within a row
- wo_shard: float32 [2048, 2048], P('tensor', 'dp'), may hold values from -0.125 to 0.125
- norm_gain: float32 [2048], replicated, may hold values from 0.1 to 1.9
- gate_shard: float32 [16, 2048, 256], P('tensor', 'dp'), may hold values from -0.125 to 0.125
- up_shard: float32 [16, 2048, 256], P('tensor', 'dp'), may hold values from -0.125 to 0.125
- down_shard: float32 [16, 256, 2048], P('tensor', None, 'dp'), may hold values from -0.1875 to 0.1875
- routes: int32 [65536, 8], P(('dp', 'tensor')), may hold values from 0 to 63, as said below
- route_weights: float32 [65536, 8], P(('dp', 'tensor')), may hold values from 0.05 to 0.3
Outputs:
- hidden_mid: bfloat16 [65536, 2048], P(('dp', 'tensor'))
- expert_sum: bfloat16 [65536, 2048], P(('dp', 'tensor'))
- key_pages: bfloat16 [544, 128, 2048], P('dp', None, 'tensor')
- value_pages: bfloat16 [544, 128, 2048], P('dp', None, 'tensor')
Inputs may be any that keep to these rules, and one draw needn't show every extreme that they name: `routes`: each row names 8 different experts. Within each aligned block of 128 rows (the rows of one device), each expert below 4 is named by 1 to 16 rows; one of them, the same in all blocks of a draw, by exactly 16 rows in every block, the others by at most 8 rows.
All inputs are finite; a program needn't handle non-finite values.
Results may differ from a plain program's by a relative error of at most 0.015.
Values may be sent and summed in bfloat16 or wider, within the bound.
No kernel may reach another device: no remote copies, remote signals or barrier semaphores. Data moves between devices by JAX's collectives and lax.ppermute only.
A program may use at most 64 MiB of HBM per device.

v0:
```python
import math
import jax
import jax.numpy as jnp
from jax import lax
from jax.sharding import PartitionSpec as P

D = 2048
HEADS = 16
HD = 128
SPLIT = 4
PAGE = 128
MOST = 16


def page_layout(lens_row, order_row, group_rows, pool_size):
    index_rows = jnp.arange(group_rows, dtype=jnp.int32)
    prompt_ends = jnp.cumsum(lens_row)
    segment = jnp.sum((index_rows[:, None] >= prompt_ends[None, :]).astype(jnp.int32), axis=1)
    prompt_starts = prompt_ends - lens_row
    owner_mask = (
        segment[:, None] == jnp.arange(lens_row.shape[0], dtype=jnp.int32)[None, :]
    ).astype(jnp.int32)
    begins = jnp.sum(owner_mask * prompt_starts[None, :], axis=1)
    page_count = (lens_row + PAGE - 1) // PAGE
    first_page = jnp.cumsum(page_count) - page_count
    page_first = jnp.sum(owner_mask * first_page[None, :], axis=1)
    position = index_rows - begins
    logical = page_first + position // PAGE
    matched = (logical[:, None] == jnp.arange(pool_size, dtype=jnp.int32)[None, :]).astype(
        jnp.int32
    )
    physical = jnp.sum(matched * order_row[None, :], axis=1)
    return (segment, physical * PAGE + position % PAGE)


def attend_group(q_heads, k_heads, v_heads, segment, heads_here):
    group_rows = q_heads.shape[0]
    block_rows = min(512, group_rows)
    count_blocks = group_rows // block_rows
    q_blocks = q_heads.reshape(count_blocks, block_rows, heads_here, HD)
    seg_blocks = segment.reshape(count_blocks, block_rows)
    k_split = k_heads.reshape(group_rows, heads_here, HD)
    v_split = v_heads.reshape(group_rows, heads_here, HD)

    def one_block(block_pair):
        q_block, seg_block = block_pair
        scores = jnp.einsum(
            "qhd,khd->hqk", q_block, k_split, preferred_element_type=jnp.float32
        ) / math.sqrt(HD)
        same_prompt = seg_block[:, None] == segment[None, :]
        scores = jnp.where(same_prompt[None, :, :], scores, -jnp.inf)
        row_max = jnp.max(scores, axis=2, keepdims=True)
        weights = jnp.exp(scores - row_max)
        totals = jnp.sum(weights, axis=2)
        output = jnp.einsum(
            "hqk,khd->qhd",
            weights.astype(jnp.bfloat16),
            v_split,
            preferred_element_type=jnp.float32,
        )
        output = output / jnp.transpose(totals)[:, :, None]
        return output.astype(jnp.bfloat16).reshape(block_rows, heads_here * HD)

    return lax.map(one_block, (q_blocks, seg_blocks)).reshape(group_rows, heads_here * HD)


def body(
    residual,
    queries,
    new_keys,
    new_values,
    lengths,
    page_order,
    wo_shard,
    norm_gain,
    gate_shard,
    up_shard,
    down_shard,
    routes,
    route_weights,
):
    tensor_count = lax.axis_size("tensor")
    heads_here = HEADS // tensor_count
    q_heads, k_heads, v_heads = (
        lax.all_to_all(queries, "tensor", split_axis=1, concat_axis=0, tiled=True),
        lax.all_to_all(new_keys, "tensor", split_axis=1, concat_axis=0, tiled=True),
        lax.all_to_all(new_values, "tensor", split_axis=1, concat_axis=0, tiled=True),
    )
    group_rows = q_heads.shape[0]
    pool_size = page_order.shape[1]
    segment, slot_index = page_layout(lengths[0], page_order[0], group_rows, pool_size)
    head_width = k_heads.shape[1]
    key_pages = (
        jnp.zeros((pool_size * PAGE, head_width), jnp.bfloat16)
        .at[slot_index]
        .set(k_heads)
        .reshape(pool_size, PAGE, head_width)
    )
    value_pages = (
        jnp.zeros((pool_size * PAGE, head_width), jnp.bfloat16)
        .at[slot_index]
        .set(v_heads)
        .reshape(pool_size, PAGE, head_width)
    )
    attended = attend_group(q_heads, k_heads, v_heads, segment, heads_here)
    token_rows = lax.all_to_all(attended, "tensor", split_axis=0, concat_axis=1, tiled=True)
    wo_cast = wo_shard.astype(jnp.bfloat16)
    columns = lax.all_gather(wo_cast, "dp", axis=1, tiled=True)
    projected = jnp.dot(
        token_rows,
        lax.all_gather(columns, "tensor", axis=0, tiled=True),
        preferred_element_type=jnp.float32,
    )
    hidden_mid = (residual.astype(jnp.float32) + projected).astype(jnp.bfloat16)
    mid_float = hidden_mid.astype(jnp.float32)
    normed = (
        mid_float
        * lax.rsqrt(jnp.mean(mid_float * mid_float, axis=1, keepdims=True) + 1e-06)
        * norm_gain
    ).astype(jnp.bfloat16)
    flight = tensor_count // SPLIT
    flight_ids = jnp.arange(flight, dtype=jnp.int32)
    named_here = routes[:, :, None] == flight_ids[None, None, :]
    routed = jnp.any(named_here, axis=1)
    weight_sum = jnp.sum(jnp.where(named_here, route_weights[:, :, None], 0.0), axis=1)
    ranked = jnp.cumsum(routed.astype(jnp.int32), axis=0) - 1
    picked = (ranked[:, :, None] == jnp.arange(MOST, dtype=jnp.int32)[None, None, :]) & routed[
        :, :, None
    ]
    outgoing = jnp.einsum(
        "tem,td->emd", picked.astype(jnp.bfloat16), normed, preferred_element_type=jnp.float32
    ).astype(jnp.bfloat16)
    outgoing = jnp.repeat(outgoing, SPLIT, axis=0)
    gate_full, up_full, down_full = (
        lax.all_gather(gate_shard.astype(jnp.bfloat16), "dp", axis=1, tiled=True),
        lax.all_gather(up_shard.astype(jnp.bfloat16), "dp", axis=1, tiled=True),
        lax.all_gather(down_shard.astype(jnp.bfloat16), "dp", axis=2, tiled=True),
    )
    arrived = lax.all_to_all(outgoing, "tensor", split_axis=0, concat_axis=0, tiled=True)
    gate_val = jnp.einsum("smd,dp->smp", arrived, gate_full[0], preferred_element_type=jnp.float32)
    up_val = jnp.einsum("smd,dp->smp", arrived, up_full[0], preferred_element_type=jnp.float32)
    inner_act = (jax.nn.silu(gate_val) * up_val).astype(jnp.bfloat16)
    result = jnp.einsum(
        "smp,pd->smd", inner_act, down_full[0], preferred_element_type=jnp.float32
    ).astype(jnp.bfloat16)
    returned = lax.all_to_all(result, "tensor", split_axis=0, concat_axis=0, tiled=True)
    summed = jnp.sum(returned.reshape(flight, SPLIT, MOST, D).astype(jnp.float32), axis=1)
    mixing = picked.astype(jnp.float32) * weight_sum[:, :, None]
    expert_sum = jnp.einsum("tem,emd->td", mixing, summed, precision=lax.Precision.HIGHEST).astype(
        jnp.bfloat16
    )
    return (hidden_mid, expert_sum, key_pages, value_pages)


def solution(mesh):
    return jax.shard_map(
        body,
        mesh=mesh,
        in_specs=(
            P(("dp", "tensor"), None),
            P(("dp", "tensor"), None),
            P(("dp", "tensor"), None),
            P(("dp", "tensor"), None),
            P("dp", None),
            P("dp", None),
            P("tensor", "dp"),
            P(),
            P("tensor", "dp", None),
            P("tensor", "dp", None),
            P("tensor", None, "dp"),
            P(("dp", "tensor"), None),
            P(("dp", "tensor"), None),
        ),
        out_specs=(
            P(("dp", "tensor"), None),
            P(("dp", "tensor"), None),
            P("dp", None, "tensor"),
            P("dp", None, "tensor"),
        ),
        check_vma=False,
    )
```

profile of v0, /device:TPU:1, one launch (start us, length us, event | category | flops | bytes accessed | tf_op | source)
XLA Modules:
  0.0 635.9 jit_solution(6192346306838084614)
XLA Ops:
  7.2 0.0 all-gather.5.cloned.1.call-start
  7.2 0.8 convert_element_type.68
  8.1 77.1 %all_gather.15 = bf16[128,2048]{0,1:T(8,128)(2,1)} all-gather(bf16[128,64]{0,1:T(8,128)(2,1)S(1)} %convert_element_type.68), channel_id=1, replica_groups=mesh['dp'=32,'tensor'=16] {'dp'}, dimensions={1}, use_global_device_ids=true | all-gather | bytes 540672 | tf_op jit(solution)/shard_map/all_gather | solution.py:108
  85.1 0.0 all-gather.5.cloned.1.call-update
  85.2 0.0 all-gather.7.cloned.1.call-start
  85.2 1.4 convert_element_type.74
  86.7 0.0 all-gather.7.cloned.1.call-update
  86.7 2.0 copy.76
  88.7 19.2 %all-to-all-start.1 = ((bf16[128,16,128]{0,2,1:T(8,128)(2,1)}), bf16[128,16,128]{0,2,1:T(8,128)(2,1)S(1)}, u32[]{:S(2)}, u32[]{:S(2)}) async-start(bf16[128,16,128]{0,2,1:T(8,128)(2,1)} %bitcast.14), calls=%async_computation.1 | async-start | bytes 1048576 | tf_op jit(solution)/shard_map/all_to_all | solution.py:86
  107.9 2.0 copy.78
  109.9 9.6 %all-to-all-done.1 = bf16[128,16,128]{0,2,1:T(8,128)(2,1)S(1)} async-done(((bf16[128,16,128]{0,2,1:T(8,128)(2,1)}), bf16[128,16,128]{0,2,1:T(8,128)(2,1)S(1)}, u32[]{:S(2)}, u32[]{:S(2)}) %all-to-all-start.1) | async-done | bytes 524320 | tf_op jit(solution)/shard_map/all_to_all | solution.py:86
  119.5 4.6 all-to-all-start.2
  124.1 1.0 copy.74
  125.1 12.6 %all-to-all-done.2 = bf16[128,16,128]{0,2,1:T(8,128)(2,1)S(1)} async-done(((bf16[128,16,128]{0,2,1:T(8,128)(2,1)}), bf16[128,16,128]{0,2,1:T(8,128)(2,1)S(1)}, u32[]{:S(2)}, u32[]{:S(2)}) %all-to-all-start.2) | async-done | bytes 524320 | tf_op jit(solution)/shard_map/all_to_all | solution.py:87
  137.8 5.7 all-to-all-start
  143.5 0.0 all-gather.11.cloned.1.call-start
  143.5 0.6 convert_element_type.77
  144.2 0.1 all-gather.11.cloned.1.call-update
  144.2 0.2 reduce-window.6
  144.4 0.1 fusion.54
  144.5 0.3 copy.77
  144.8 0.3 copy.79
  145.1 11.8 %all-to-all-done = bf16[128,16,128]{0,2,1:T(8,128)(2,1)S(1)} async-done(((bf16[128,16,128]{0,2,1:T(8,128)(2,1)}), bf16[128,16,128]{0,2,1:T(8,128)(2,1)S(1)}, u32[]{:S(2)}, u32[]{:S(2)}) %all-to-all-start) | async-done | bytes 524320 | tf_op jit(solution)/shard_map/all_to_all | solution.py:85
  156.9 0.3 copy.75
  157.2 12.3 %while.10 = (s32[]{:T(128)}, bf16[4,512,128]{2,1,0:T(8,128)(2,1)}, s32[4,512]{1,0:T(4,128)S(1)}, s32[2048]{0:T(1024)S(1)}, bf16[4,512,1,128]{3,1,2,0:T(8,128)(2,...) while((s32[]{:T(128)}, bf16[4,512,128]{2,1,0:T(8,128)(2,1)}, ...), condition=%wide.region_5.6_spmd, body=%wide.region_2.0_spmd.sunk | while | flops 545389568 | bytes 13918813 | solution.py:64
  157.2 0.9 fusion.83
  158.1 0.7 fusion.84
  158.8 1.5 fusion.85
  160.3 0.9 fusion.83
  161.2 0.7 fusion.84
  161.9 1.4 fusion.85
  163.4 0.9 fusion.83
  164.3 0.7 fusion.84
  165.0 1.5 fusion.85
  166.4 0.9 fusion.83
  167.3 0.7 fusion.84
  168.0 1.5 fusion.85
  169.5 4.9 all-to-all-start.3
  174.4 0.0 all-gather.9.cloned.1.call-start
  174.4 0.6 convert_element_type.75
  175.1 0.1 copy.82
  175.2 0.2 reduce_window_sum.20
  175.4 0.1 copy.83
  175.5 8.6 %all-to-all-done.3 = bf16[16,128,128]{2,1,0:T(8,128)(2,1)S(1)} async-done(((bf16[16,128,128]{2,1,0:T(8,128)(2,1)}), bf16[16,128,128]{2,1,0:T(8,128)(2,1)S(1)}, u32[]{:S(2)}, u32[]{:S(2)}) %all-to-all-start.3) | async-done | bytes 524320 | tf_op jit(solution)/shard_map/all_to_all | solution.py:106
  184.1 0.3 copy.81
  184.4 0.0 all-gather.5.cloned.1.call-done
  184.4 6.4 %fusion.28 = (f32[128]{0:T(128)S(1)}, bf16[128,2048]{1,0:T(8,128)(2,1)S(1)}) fusion(bf16[128,2048]{0,1:T(8,128)(2,1)S(1)} %bitcast.108, bf16[2048,2048]{0,1:T(8,128)(2,1)} %all-gather.5.cloned.1.call-done, bf16[128,2048]{1,0:T(8,128)(2,1)S(1)} %copy-done), kind=kOutput, calls=%fused_computation.30 | convolution fusion | flops 1075314560 | bytes 9961984 | tf_op jit(solution)/shard_map/dot_general | solution.py:109
  190.8 0.3 convolution_convert_fusion.1
  191.2 1.1 broadcast_in_dim.27
  192.3 4.7 all-to-all-start.4
  197.0 0.2 reduce-window_1_clone.1
  197.2 0.1 select_reduce_fusion.1
  197.3 114.6 %all-gather.7.cloned.1.call-done = bf16[1,2048,256]{2,1,0:T(8,128)(2,1)} async-done(((bf16[1,64,256]{2,1,0:T(8,128)(2,1)}), bf16[1,2048,256]{2,1,0:T(8,128)(2,1)}) %all-gather.7.cloned.1.call-update) | async-done | bytes 1048592 | tf_op jit(solution)/shard_map/all_gather | solution.py:135
  311.9 1.7 fusion.34
  313.6 139.5 %all-gather.11.cloned.1.call-done = bf16[1,256,2048]{1,2,0:T(8,128)(2,1)} async-done(((bf16[1,256,64]{1,2,0:T(8,128)(2,1)}), bf16[1,256,2048]{1,2,0:T(8,128)(2,1)}) %all-gather.11.cloned.1.call-update) | async-done | bytes 1048592 | tf_op jit(solution)/shard_map/all_gather | solution.py:137
  453.0 141.0 %all-gather.9.cloned.1.call-done = bf16[1,2048,256]{2,1,0:T(8,128)(2,1)} async-done(((bf16[1,64,256]{2,1,0:T(8,128)(2,1)}), bf16[1,2048,256]{2,1,0:T(8,128)(2,1)}) %all-gather.9.cloned.1.call-update) | async-done | bytes 1048592 | tf_op jit(solution)/shard_map/all_gather | solution.py:136
  594.0 3.8 convolution_convert_fusion
  597.8 14.0 %all-to-all-start.5 = ((bf16[16,16,2048]{2,1,0:T(8,128)(2,1)}), bf16[16,16,2048]{2,1,0:T(8,128)(2,1)S(1)}, u32[]{:S(2)}, u32[]{:S(2)}) async-start(bf16[16,16,2048]{2,1,0:T(8,128)(2,1)} %convolution_convert_fusion), calls=%async_computation.5 | async-start | bytes 2097152 | tf_op jit(solution)/shard_map/all_to_all | solution.py:146
  611.9 0.1 select_reduce_fusion
  612.1 6.5 %scatter_custom_fusion = bf16[2176,128]{1,0:T(8,128)(2,1)} fusion(s32[2048]{0:T(1024)S(1)} %bitcast.121, bf16[2048,128]{1,0:T(8,128)(2,1)S(1)} %bitcast.116, bf16[]{:T(256)} %constant.81.clone.1), kind=kCustom, calls=%fused_computation.42 | custom fusion | bytes 557058 | tf_op jit(solution)/shard_map/scatter | solution.py:96
  618.6 6.5 %scatter_custom_fusion.1 = bf16[2176,128]{1,0:T(8,128)(2,1)} fusion(s32[2048]{0:T(1024)S(1)} %bitcast.122, bf16[2048,128]{1,0:T(8,128)(2,1)S(1)} %bitcast.107, bf16[]{:T(256)} %constant.81.clone.1), kind=kCustom, calls=%fused_computation.40 | custom fusion | bytes 557058 | tf_op jit(solution)/shard_map/scatter | solution.py:102
  625.2 2.2 all-to-all-done.5
  627.3 0.2 convert_reduce_fusion
  627.5 1.8 fusion.26
  (38 shorter events, 0.2 us)
Async XLA Ops:
  7.2 116.9 %copy-start.2 = (bf16[128,2048]{1,0:T(8,128)(2,1)S(1)}, bf16[128,2048]{1,0:T(8,128)(2,1)}, u32[]{:S(2)}) copy-start(bf16[128,2048]{1,0:T(8,128)(2,1)} %param.16) | copy-start | bytes 1572868
  7.2 136.3 %copy-start.3 = (f32[1,256,64]{1,2,0:T(8,128)S(1)}, f32[1,256,64]{1,2,0:T(8,128)}, u32[]{:S(2)}) copy-start(f32[1,256,64]{1,2,0:T(8,128)} %param.25) | copy-start | bytes 196612
  7.2 137.0 %copy-start.8 = (s32[1,2]{1,0:T(1,128)S(1)}, s32[1,2]{1,0:T(1,128)}, u32[]{:S(2)}) copy-start(s32[1,2]{1,0:T(1,128)} %param.19) | copy-start | bytes 28
  7.2 177.2 %all-gather.5.cloned.1.call-start = ((), (), s32[]{:S(2)}) async-start(), calls=%async_computation.6 | async-start | bytes 8912896 | tf_op jit(solution)/shard_map/all_gather | solution.py:111
  85.2 226.8 %all-gather.7.cloned.1.call-start = ((), (), s32[]{:S(2)}) async-start(), calls=%async_computation.7 | async-start | bytes 1081344 | tf_op jit(solution)/shard_map/all_gather | solution.py:135
  88.7 30.8 %all-to-all-start.1 = ((bf16[128,16,128]{0,2,1:T(8,128)(2,1)}), bf16[128,16,128]{0,2,1:T(8,128)(2,1)S(1)}, u32[]{:S(2)}, u32[]{:S(2)}) async-start(bf16[128,16,128]{0,2,1:T(8,128)(2,1)} %bitcast.14), calls=%async_computation.1 | async-start | bytes 1048576 | tf_op jit(solution)/shard_map/all_to_all | solution.py:86
  119.5 18.2 %all-to-all-start.2 = ((bf16[128,16,128]{0,2,1:T(8,128)(2,1)}), bf16[128,16,128]{0,2,1:T(8,128)(2,1)S(1)}, u32[]{:S(2)}, u32[]{:S(2)}) async-start(bf16[128,16,128]{0,2,1:T(8,128)(2,1)} %bitcast.17), calls=%async_computation.2 | async-start | bytes 1048576 | tf_op jit(solution)/shard_map/all_to_all | solution.py:87
  137.8 19.1 %all-to-all-start = ((bf16[128,16,128]{0,2,1:T(8,128)(2,1)}), bf16[128,16,128]{0,2,1:T(8,128)(2,1)S(1)}, u32[]{:S(2)}, u32[]{:S(2)}) async-start(bf16[128,16,128]{0,2,1:T(8,128)(2,1)} %bitcast.10), calls=%async_computation | async-start | bytes 1048576 | tf_op jit(solution)/shard_map/all_to_all | solution.py:85
  143.5 309.6 %all-gather.11.cloned.1.call-start = ((), (), s32[]{:S(2)}) async-start(), calls=%async_computation.9 | async-start | bytes 1081344 | tf_op jit(solution)/shard_map/all_gather | solution.py:137
  157.1 17.3 %copy-start.4 = (f32[1,64,256]{2,1,0:T(8,128)S(1)}, f32[1,64,256]{2,1,0:T(8,128)}, u32[]{:S(2)}) copy-start(f32[1,64,256]{2,1,0:T(8,128)} %param.24) | copy-start | bytes 196612
  157.2 17.9 %copy-start.5 = (s32[128,8]{0,1:T(8,128)S(1)}, s32[128,8]{0,1:T(8,128)}, u32[]{:S(2)}) copy-start(s32[128,8]{0,1:T(8,128)} %param.26) | copy-start | bytes 12292
  157.2 27.2 %copy-start = (bf16[128,2048]{1,0:T(8,128)(2,1)S(1)}, bf16[128,2048]{1,0:T(8,128)(2,1)}, u32[]{:S(2)}) copy-start(bf16[128,2048]{1,0:T(8,128)(2,1)} %param.15) | copy-start | bytes 1572868
  169.5 14.6 %all-to-all-start.3 = ((bf16[16,128,128]{2,1,0:T(8,128)(2,1)}), bf16[16,128,128]{2,1,0:T(8,128)(2,1)S(1)}, u32[]{:S(2)}, u32[]{:S(2)}) async-start(bf16[16,128,128]{2,1,0:T(8,128)(2,1)} %bitcast.20), calls=%async_computation.3 | async-start | bytes 1048576 | tf_op jit(solution)/shard_map/all_to_all | solution.py:106
  174.4 419.6 %all-gather.9.cloned.1.call-start = ((), (), s32[]{:S(2)}) async-start(), calls=%async_computation.8 | async-start | bytes 1081344 | tf_op jit(solution)/shard_map/all_gather | solution.py:136
  184.4 6.4 %copy-start.9 = (f32[2048]{0:T(1024)S(1)}, f32[2048]{0:T(1024)}, u32[]{:S(2)}) copy-start(f32[2048]{0:T(1024)} %param.22) | copy-start | bytes 24580
  190.8 407.1 %copy-start.1 = (bf16[128,2048]{1,0:T(8,128)(2,1)}, bf16[128,2048]{1,0:T(8,128)(2,1)S(1)}, u32[]{:S(2)}) copy-start(bf16[128,2048]{1,0:T(8,128)(2,1)S(1)} %get-tuple-element.98) | copy-start | bytes 1572868
  190.8 6.4 copy-start.6
  192.3 119.6 %all-to-all-start.4 = ((bf16[16,16,2048]{2,1,0:T(8,128)(2,1)}), bf16[16,16,2048]{2,1,0:T(8,128)(2,1)S(1)}, u32[]{:S(2)}, u32[]{:S(2)}) async-start(bf16[16,16,2048]{2,1,0:T(8,128)(2,1)} %bitcast.24), calls=%async_computation.4 | async-start | bytes 2097152 | tf_op jit(solution)/shard_map/all_to_all | solution.py:139
  197.3 414.6 %copy-start.7 = (s32[1,17]{1,0:T(1,128)S(1)}, s32[1,17]{1,0:T(1,128)}, u32[]{:S(2)}) copy-start(s32[1,17]{1,0:T(1,128)} %param.20) | copy-start | bytes 208
  597.8 29.5 %all-to-all-start.5 = ((bf16[16,16,2048]{2,1,0:T(8,128)(2,1)}), bf16[16,16,2048]{2,1,0:T(8,128)(2,1)S(1)}, u32[]{:S(2)}, u32[]{:S(2)}) async-start(bf16[16,16,2048]{2,1,0:T(8,128)(2,1)} %convolution_convert_fusion), calls=%async_computation.5 | async-start | bytes 2097152 | tf_op jit(solution)/shard_map/all_to_all | solution.py:146
Sparse Core Ops, SparseCore 0:
  85.3 89.7 all-gather.4
  178.1 133.7 all-gather.6
  315.6 137.4 all-gather.10
  456.6 137.4 all-gather.8
where the time goes:
time: 637 us; the launch traced here: 636 us
  waiting for transfers between devices  440 us (69%)
  blocking collectives  77.1 us (12%)
  starting transfers between devices  53.2 us (8%)
  matrix products  23.4 us (4%)
  local copies, waits for them, and re-layouts  20.7 us (3%)
  between operations  14 us (2%)
  other arithmetic  7.47 us (1%)
    all_gather x1, waiting for transfers between devices, body(): lax.all_gather(up_shard.astype(jnp.bfloat16), 'dp', axis=1, tiled=True)  141 us
    all_gather x1, waiting for transfers between devices, body(): lax.all_gather(down_shard.astype(jnp.bfloat16), 'dp', axis=2, tiled=True)  139 us
    all_gather x1, waiting for transfers between devices, body(): lax.all_gather(gate_shard.astype(jnp.bfloat16), 'dp', axis=1, tiled=True)  115 us
    all_gather x1, blocking collectives, body(): columns = lax.all_gather(wo_cast, 'dp', axis=1, tiled=True)  77.1 us
    all_to_all x1, starting transfers between devices, body(): lax.all_to_all(new_keys, 'tensor', split_axis=1, concat_axis=0, tiled=True)  19.2 us
    all_to_all x1, starting transfers between devices, body(): lax.all_to_all(result, 'tensor', split_axis=0, concat_axis=0, tiled=True)  14 us
  transfers between devices with their start and end apart: 10, of which 8 were waited for; matrix products, arithmetic and copies ran while one was open for 7% of the time, Pallas kernels for 0%

commit v1 on v0

--- a/solution.py
+++ b/solution.py
@@ -132,7 +132,12 @@
     ).astype(jnp.bfloat16)
     outgoing = jnp.repeat(outgoing, SPLIT, axis=0)
     gate_full, up_full, down_full = (
-        lax.all_gather(gate_shard.astype(jnp.bfloat16), "dp", axis=1, tiled=True),
+        jnp.concatenate(
+            lax.all_to_all(
+                jnp.stack([gate_shard.astype(jnp.bfloat16)] * lax.axis_size("dp")), "dp", 0, 0
+            ),
+            axis=1,
+        ),
         lax.all_gather(up_shard.astype(jnp.bfloat16), "dp", axis=1, tiled=True),
         lax.all_gather(down_shard.astype(jnp.bfloat16), "dp", axis=2, tiled=True),
     )

time: 637 us -> 517 us (0.81)
  waiting for transfers between devices: 440 us -> 316 us
    all_gather x1 -> x0, waiting for transfers between devices: 115 us -> none  [body(): lax.all_gather(gate_shard.astype(jnp.bfloat16), 'dp', axis=1, tiled=True)]
    all_gather x1, waiting for transfers between devices: 141 us -> 67.5 us  [body(): lax.all_gather(up_shard.astype(jnp.bfloat16), 'dp', axis=1, tiled=True)]
    all_to_all x0 -> x1, waiting for transfers between devices: none -> 43.5 us  [body(): lax.all_to_all(jnp.stack([gate_shard.astype(jnp.bfloat16)] * lax.axis_siz...]
    all_to_all x1, waiting for transfers between devices: 0.01 us -> 15.2 us  [body(): lax.all_to_all(outgoing, 'tensor', split_axis=0, concat_axis=0, tiled=True)]
  transfers between devices with their start and end apart: 10 -> 10, of which waited for: 8 -> 9; matrix products, arithmetic and copies ran while one was open for 7% -> 8% of each run, Pallas kernels for 0% -> 0%
where the time goes in v1:
time: 517 us; the launch traced here: 516 us
  waiting for transfers between devices  316 us (61%)
  blocking collectives  77.1 us (15%)
  starting transfers between devices  58 us (11%)
  local copies, waits for them, and re-layouts  22.9 us (4%)
  matrix products  22.3 us (4%)
  between operations  14 us (3%)
  other arithmetic  6.03 us (1%)
    all_gather x1, waiting for transfers between devices, body(): lax.all_gather(down_shard.astype(jnp.bfloat16), 'dp', axis=2, tiled=True)  141 us
    all_gather x1, blocking collectives, body(): columns = lax.all_gather(wo_cast, 'dp', axis=1, tiled=True)  77.1 us
    all_gather x1, waiting for transfers between devices, body(): lax.all_gather(up_shard.astype(jnp.bfloat16), 'dp', axis=1, tiled=True)  67.5 us
    all_to_all x1, waiting for transfers between devices, body(): lax.all_to_all(jnp.stack([gate_shard.astype(jnp.bfloat16)] * lax.axis_siz...  43.5 us
    all_to_all x1, starting transfers between devices, body(): lax.all_to_all(new_keys, 'tensor', split_axis=1, concat_axis=0, tiled=True)  19.2 us
    all_to_all x1, waiting for transfers between devices, body(): lax.all_to_all(outgoing, 'tensor', split_axis=0, concat_axis=0, tiled=True)  15.2 us
    all_to_all x1, starting transfers between devices, body(): lax.all_to_all(result, 'tensor', split_axis=0, concat_axis=0, tiled=True)  14 us
    all_to_all x1, waiting for transfers between devices, body(): lax.all_to_all(queries, 'tensor', split_axis=1, concat_axis=0, tiled=True)  13 us
  transfers between devices with their start and end apart: 10, of which 9 were waited for; matrix products, arithmetic and copies ran while one was open for 8% of the time, Pallas kernels for 0%

profile of v1, /device:TPU:1, one launch (start us, length us, event | category | flops | bytes accessed | tf_op | source)
XLA Modules:
  0.0 516.0 jit_solution(8717750398816490362)
XLA Ops:
  7.2 0.0 all-gather.4.cloned.1.call-start
  7.2 0.8 convert_element_type.70
  8.0 77.1 %all_gather.12 = bf16[128,2048]{0,1:T(8,128)(2,1)} all-gather(bf16[128,64]{0,1:T(8,128)(2,1)S(1)} %convert_element_type.70), channel_id=1, replica_groups=mesh['dp'=32,'tensor'=16] {'dp'}, dimensions={1}, use_global_device_ids=true | all-gather | bytes 540672 | tf_op jit(solution)/shard_map/all_gather | solution.py:108
  85.1 2.0 copy.76
  87.2 19.2 %all-to-all-start.1 = ((bf16[128,16,128]{0,2,1:T(8,128)(2,1)}), bf16[128,16,128]{0,2,1:T(8,128)(2,1)S(1)}, u32[]{:S(2)}, u32[]{:S(2)}) async-start(bf16[128,16,128]{0,2,1:T(8,128)(2,1)} %bitcast.14), calls=%async_computation.1 | async-start | bytes 1048576 | tf_op jit(solution)/shard_map/all_to_all | solution.py:86
  106.3 2.0 copy.78
  108.4 11.2 %all-to-all-done.1 = bf16[128,16,128]{0,2,1:T(8,128)(2,1)S(1)} async-done(((bf16[128,16,128]{0,2,1:T(8,128)(2,1)}), bf16[128,16,128]{0,2,1:T(8,128)(2,1)S(1)}, u32[]{:S(2)}, u32[]{:S(2)}) %all-to-all-start.1) | async-done | bytes 524320 | tf_op jit(solution)/shard_map/all_to_all | solution.py:86
  119.6 4.2 all-to-all-start.2
  123.8 1.0 copy.74
  124.8 12.5 %all-to-all-done.2 = bf16[128,16,128]{0,2,1:T(8,128)(2,1)S(1)} async-done(((bf16[128,16,128]{0,2,1:T(8,128)(2,1)}), bf16[128,16,128]{0,2,1:T(8,128)(2,1)S(1)}, u32[]{:S(2)}, u32[]{:S(2)}) %all-to-all-start.2) | async-done | bytes 524320 | tf_op jit(solution)/shard_map/all_to_all | solution.py:87
  137.3 4.8 all-to-all-start
  142.1 0.2 reduce-window.6
  142.3 0.1 fusion.52
  142.4 0.3 copy.77
  142.7 0.3 copy.79
  143.0 13.0 %all-to-all-done = bf16[128,16,128]{0,2,1:T(8,128)(2,1)S(1)} async-done(((bf16[128,16,128]{0,2,1:T(8,128)(2,1)}), bf16[128,16,128]{0,2,1:T(8,128)(2,1)S(1)}, u32[]{:S(2)}, u32[]{:S(2)}) %all-to-all-start) | async-done | bytes 524320 | tf_op jit(solution)/shard_map/all_to_all | solution.py:85
  156.0 0.3 copy.75
  156.3 12.3 %while.10 = (s32[]{:T(128)}, bf16[4,512,128]{2,1,0:T(8,128)(2,1)}, s32[4,512]{1,0:T(4,128)S(1)}, s32[2048]{0:T(1024)S(1)}, bf16[4,512,1,128]{3,1,2,0:T(8,128)(2,...) while((s32[]{:T(128)}, bf16[4,512,128]{2,1,0:T(8,128)(2,1)}, ...), condition=%wide.region_5.6_spmd, body=%wide.region_2.0_spmd.sunk | while | flops 545389568 | bytes 13918813 | solution.py:64
  156.3 0.9 fusion.83
  157.2 0.7 fusion.84
  157.9 1.5 fusion.85
  159.4 0.9 fusion.83
  160.3 0.7 fusion.84
  161.0 1.5 fusion.85
  162.5 0.9 fusion.83
  163.4 0.7 fusion.84
  164.1 1.5 fusion.85
  165.5 0.9 fusion.83
  166.4 0.7 fusion.84
  167.1 1.4 fusion.85
  168.6 0.8 copy-done.3
  169.4 5.4 %all-to-all-start.3 = ((bf16[16,128,128]{2,1,0:T(8,128)(2,1)}), bf16[16,128,128]{2,1,0:T(8,128)(2,1)S(1)}, u32[]{:S(2)}, u32[]{:S(2)}) async-start(bf16[16,128,128]{2,1,0:T(8,128)(2,1)} %bitcast.20), calls=%async_computation.3 | async-start | bytes 1048576 | tf_op jit(solution)/shard_map/all_to_all | solution.py:106
  174.8 9.7 %all-to-all-done.3 = bf16[16,128,128]{2,1,0:T(8,128)(2,1)S(1)} async-done(((bf16[16,128,128]{2,1,0:T(8,128)(2,1)}), bf16[16,128,128]{2,1,0:T(8,128)(2,1)S(1)}, u32[]{:S(2)}, u32[]{:S(2)}) %all-to-all-start.3) | async-done | bytes 524320 | tf_op jit(solution)/shard_map/all_to_all | solution.py:106
  184.5 1.1 stack.2
  185.6 4.1 all-to-all-start.5
  189.7 0.0 all-gather.6.cloned.1.call-start
  189.8 0.6 convert_element_type.78
  190.4 0.1 all-gather.6.cloned.1.call-update
  190.5 0.0 all-gather.8.cloned.1.call-start
  190.5 0.6 convert_element_type.80
  191.2 0.1 all-gather.8.cloned.1.call-update
  191.3 0.1 copy.82
  191.4 0.2 reduce_window_sum.20
  191.6 0.1 copy.83
  191.6 0.3 copy.81
  192.0 6.4 %fusion.28 = (f32[128]{0:T(128)S(1)}, bf16[128,2048]{1,0:T(8,128)(2,1)S(1)}) fusion(bf16[128,2048]{0,1:T(8,128)(2,1)S(1)} %bitcast.111, bf16[2048,2048]{0,1:T(8,128)(2,1)} %all-gather.4.cloned.1.call-done, bf16[128,2048]{1,0:T(8,128)(2,1)S(1)} %copy-done), kind=kOutput, calls=%fused_computation.30 | convolution fusion | flops 1075314560 | bytes 9961984 | tf_op jit(solution)/shard_map/dot_general | solution.py:109
  198.4 0.3 convolution_convert_fusion.1
  198.8 43.5 %all-to-all-done.5 = bf16[32,1,64,256]{3,2,1,0:T(8,128)(2,1)S(1)} async-done(((bf16[32,1,64,256]{3,2,1,0:T(8,128)(2,1)}), bf16[32,1,64,256]{3,2,1,0:T(8,128)(2,1)S(1)}, u32[]{:S(2)}, u32[]{:S(2)}) %all-to-all-start.5) | async-done | bytes 1048608 | tf_op jit(solution)/shard_map/all_to_all | solution.py:136
  242.3 1.1 broadcast_in_dim.27
  243.4 6.1 %all-to-all-start.4 = ((bf16[16,16,2048]{2,1,0:T(8,128)(2,1)}), bf16[16,16,2048]{2,1,0:T(8,128)(2,1)S(1)}, u32[]{:S(2)}, u32[]{:S(2)}) async-start(bf16[16,16,2048]{2,1,0:T(8,128)(2,1)} %bitcast.24), calls=%async_computation.4 | async-start | bytes 2097152 | tf_op jit(solution)/shard_map/all_to_all | solution.py:144
  249.5 0.2 reduce-window_1_clone.1
  249.7 0.1 select_reduce_fusion.1
  249.8 15.2 %all-to-all-done.4 = bf16[16,16,2048]{2,1,0:T(8,128)(2,1)S(1)} async-done(((bf16[16,16,2048]{2,1,0:T(8,128)(2,1)}), bf16[16,16,2048]{2,1,0:T(8,128)(2,1)S(1)}, u32[]{:S(2)}, u32[]{:S(2)}) %all-to-all-start.4) | async-done | bytes 1048608 | tf_op jit(solution)/shard_map/all_to_all | solution.py:144
  265.1 0.5 fusion.69
  265.5 67.5 %all-gather.6.cloned.1.call-done = bf16[1,2048,256]{2,1,0:T(8,128)(2,1)} async-done(((bf16[1,64,256]{2,1,0:T(8,128)(2,1)}), bf16[1,2048,256]{2,1,0:T(8,128)(2,1)}) %all-gather.6.cloned.1.call-update) | async-done | bytes 1048592 | tf_op jit(solution)/shard_map/all_gather | solution.py:141
  333.1 141.1 %all-gather.8.cloned.1.call-done = bf16[1,256,2048]{1,2,0:T(8,128)(2,1)} async-done(((bf16[1,256,64]{1,2,0:T(8,128)(2,1)}), bf16[1,256,2048]{1,2,0:T(8,128)(2,1)}) %all-gather.8.cloned.1.call-update) | async-done | bytes 1048592 | tf_op jit(solution)/shard_map/all_gather | solution.py:142
  474.2 3.8 convolution_convert_fusion
  478.0 14.0 %all-to-all-start.6 = ((bf16[16,16,2048]{2,1,0:T(8,128)(2,1)}), bf16[16,16,2048]{2,1,0:T(8,128)(2,1)S(1)}, u32[]{:S(2)}, u32[]{:S(2)}) async-start(bf16[16,16,2048]{2,1,0:T(8,128)(2,1)} %convolution_convert_fusion), calls=%async_computation.6 | async-start | bytes 2097152 | tf_op jit(solution)/shard_map/all_to_all | solution.py:151
  492.1 0.1 select_reduce_fusion
  492.3 6.9 %scatter_custom_fusion = bf16[2176,128]{1,0:T(8,128)(2,1)} fusion(s32[2048]{0:T(1024)S(1)} %bitcast.124, bf16[2048,128]{1,0:T(8,128)(2,1)} %bitcast.119, bf16[]{:T(256)} %constant.81.clone.1), kind=kCustom, calls=%fused_computation.40 | custom fusion | bytes 557568 | tf_op jit(solution)/shard_map/scatter | solution.py:96
  499.1 6.5 %scatter_custom_fusion.1 = bf16[2176,128]{1,0:T(8,128)(2,1)} fusion(s32[2048]{0:T(1024)S(1)} %bitcast.125, bf16[2048,128]{1,0:T(8,128)(2,1)S(1)} %bitcast.109, bf16[]{:T(256)} %constant.81.clone.1), kind=kCustom, calls=%fused_computation.38 | custom fusion | bytes 557058 | tf_op jit(solution)/shard_map/scatter | solution.py:102
  505.7 1.8 all-to-all-done.6
  507.5 0.2 convert_reduce_fusion
  507.7 1.8 fusion.26
  (42 shorter events, 0.3 us)
Async XLA Ops:
  7.2 116.6 %copy-start.2 = (bf16[128,2048]{1,0:T(8,128)(2,1)S(1)}, bf16[128,2048]{1,0:T(8,128)(2,1)}, u32[]{:S(2)}) copy-start(bf16[128,2048]{1,0:T(8,128)(2,1)} %param.16) | copy-start | bytes 1572868
  7.2 134.9 %copy-start.10 = (s32[1,2]{1,0:T(1,128)S(1)}, s32[1,2]{1,0:T(1,128)}, u32[]{:S(2)}) copy-start(s32[1,2]{1,0:T(1,128)} %param.19) | copy-start | bytes 28
  7.2 184.8 %all-gather.4.cloned.1.call-start = ((), (), s32[]{:S(2)}) async-start(), calls=%async_computation.7 | async-start | bytes 8912896 | tf_op jit(solution)/shard_map/all_gather | solution.py:111
  87.2 32.4 %all-to-all-start.1 = ((bf16[128,16,128]{0,2,1:T(8,128)(2,1)}), bf16[128,16,128]{0,2,1:T(8,128)(2,1)S(1)}, u32[]{:S(2)}, u32[]{:S(2)}) async-start(bf16[128,16,128]{0,2,1:T(8,128)(2,1)} %bitcast.14), calls=%async_computation.1 | async-start | bytes 1048576 | tf_op jit(solution)/shard_map/all_to_all | solution.py:86
  119.6 17.7 %all-to-all-start.2 = ((bf16[128,16,128]{0,2,1:T(8,128)(2,1)}), bf16[128,16,128]{0,2,1:T(8,128)(2,1)S(1)}, u32[]{:S(2)}, u32[]{:S(2)}) async-start(bf16[128,16,128]{0,2,1:T(8,128)(2,1)} %bitcast.17), calls=%async_computation.2 | async-start | bytes 1048576 | tf_op jit(solution)/shard_map/all_to_all | solution.py:87
  137.3 18.7 %all-to-all-start = ((bf16[128,16,128]{0,2,1:T(8,128)(2,1)}), bf16[128,16,128]{0,2,1:T(8,128)(2,1)S(1)}, u32[]{:S(2)}, u32[]{:S(2)}) async-start(bf16[128,16,128]{0,2,1:T(8,128)(2,1)} %bitcast.10), calls=%async_computation | async-start | bytes 1048576 | tf_op jit(solution)/shard_map/all_to_all | solution.py:85
  156.3 18.5 %copy-start.4 = (f32[1,64,256]{2,1,0:T(8,128)S(1)}, f32[1,64,256]{2,1,0:T(8,128)}, u32[]{:S(2)}) copy-start(f32[1,64,256]{2,1,0:T(8,128)} %param.23) | copy-start | bytes 196612
  168.6 0.8 copy-start.3
  168.6 21.2 %copy-start.5 = (f32[1,64,256]{2,1,0:T(8,128)S(1)}, f32[1,64,256]{2,1,0:T(8,128)}, u32[]{:S(2)}) copy-start(f32[1,64,256]{2,1,0:T(8,128)} %param.24) | copy-start | bytes 196612
  168.6 21.9 %copy-start.6 = (f32[1,256,64]{1,2,0:T(8,128)S(1)}, f32[1,256,64]{1,2,0:T(8,128)}, u32[]{:S(2)}) copy-start(f32[1,256,64]{1,2,0:T(8,128)} %param.25) | copy-start | bytes 196612
  168.6 22.6 %copy-start.7 = (s32[128,8]{0,1:T(8,128)S(1)}, s32[128,8]{0,1:T(8,128)}, u32[]{:S(2)}) copy-start(s32[128,8]{0,1:T(8,128)} %param.26) | copy-start | bytes 12292
  168.6 23.4 %copy-start = (bf16[128,2048]{1,0:T(8,128)(2,1)S(1)}, bf16[128,2048]{1,0:T(8,128)(2,1)}, u32[]{:S(2)}) copy-start(bf16[128,2048]{1,0:T(8,128)(2,1)} %param.15) | copy-start | bytes 1572868
  169.4 15.1 %all-to-all-start.3 = ((bf16[16,128,128]{2,1,0:T(8,128)(2,1)}), bf16[16,128,128]{2,1,0:T(8,128)(2,1)S(1)}, u32[]{:S(2)}, u32[]{:S(2)}) async-start(bf16[16,128,128]{2,1,0:T(8,128)(2,1)} %bitcast.20), calls=%async_computation.3 | async-start | bytes 1048576 | tf_op jit(solution)/shard_map/all_to_all | solution.py:106
  185.6 56.7 %all-to-all-start.5 = ((bf16[32,1,64,256]{3,2,1,0:T(8,128)(2,1)}), bf16[32,1,64,256]{3,2,1,0:T(8,128)(2,1)S(1)}, u32[]{:S(2)}, u32[]{:S(2)}) async-start(bf16[32,1,64,256]{3,2,1,0:T(8,128)(2,1)} %stack.2), calls=%async_computation.5 | async-start | bytes 2097152 | tf_op jit(solution)/shard_map/all_to_all | solution.py:136
  189.7 143.3 %all-gather.6.cloned.1.call-start = ((), (), s32[]{:S(2)}) async-start(), calls=%async_computation.8 | async-start | bytes 1081344 | tf_op jit(solution)/shard_map/all_gather | solution.py:141
  190.5 283.7 %all-gather.8.cloned.1.call-start = ((), (), s32[]{:S(2)}) async-start(), calls=%async_computation.9 | async-start | bytes 1081344 | tf_op jit(solution)/shard_map/all_gather | solution.py:142
  192.0 6.5 %copy-start.11 = (f32[2048]{0:T(1024)S(1)}, f32[2048]{0:T(1024)}, u32[]{:S(2)}) copy-start(f32[2048]{0:T(1024)} %param.22) | copy-start | bytes 24580
  198.4 45.0 %copy-start.1 = (bf16[128,2048]{1,0:T(8,128)(2,1)}, bf16[128,2048]{1,0:T(8,128)(2,1)S(1)}, u32[]{:S(2)}) copy-start(bf16[128,2048]{1,0:T(8,128)(2,1)S(1)} %get-tuple-element.98) | copy-start | bytes 1572868
  198.4 51.3 %copy-start.8 = (f32[128,8]{0,1:T(8,128)S(1)}, f32[128,8]{0,1:T(8,128)}, u32[]{:S(2)}) copy-start(f32[128,8]{0,1:T(8,128)} %param.27) | copy-start | bytes 12292
  243.4 21.7 %all-to-all-start.4 = ((bf16[16,16,2048]{2,1,0:T(8,128)(2,1)}), bf16[16,16,2048]{2,1,0:T(8,128)(2,1)S(1)}, u32[]{:S(2)}, u32[]{:S(2)}) async-start(bf16[16,16,2048]{2,1,0:T(8,128)(2,1)} %bitcast.24), calls=%async_computation.4 | async-start | bytes 2097152 | tf_op jit(solution)/shard_map/all_to_all | solution.py:144
  265.1 227.0 %copy-start.9 = (s32[1,17]{1,0:T(1,128)S(1)}, s32[1,17]{1,0:T(1,128)}, u32[]{:S(2)}) copy-start(s32[1,17]{1,0:T(1,128)} %param.20) | copy-start | bytes 208
  478.0 29.5 %all-to-all-start.6 = ((bf16[16,16,2048]{2,1,0:T(8,128)(2,1)}), bf16[16,16,2048]{2,1,0:T(8,128)(2,1)S(1)}, u32[]{:S(2)}, u32[]{:S(2)}) async-start(bf16[16,16,2048]{2,1,0:T(8,128)(2,1)} %convolution_convert_fusion), calls=%async_computation.6 | async-start | bytes 2097152 | tf_op jit(solution)/shard_map/all_to_all | solution.py:151
Sparse Core Ops, SparseCore 0:
  85.3 88.2 all-gather.3
  194.2 138.7 all-gather.5
  336.8 137.4 all-gather.7
